TPU v7x, 32 devices: a whole 2x2x4 slice. The times are simulated.
32 devices in a mesh: dom: 8 (over z, y), rep: 4 (over x, core).
Axes of the slice: x: 2, y: 2, z: 4, core: 2. Of those that a mesh axis runs over, the one named last changes fastest.
Arguments:
- rhs: float32 [256, 32, 128], P(('dom', 'rep')), may hold values from -15 to 15
- precond: float32 [256, 128], P(('dom', 'rep')), may hold values from 0.25 to 1
- diag_tiles: bfloat16 [256, 128, 128], P(('dom', 'rep')), may hold values from -0.08 to 6.08
- off_tiles: bfloat16 [256, 2, 128, 128], P(('dom', 'rep')), may hold values from -0.119628906 to 0.119628906
- off_cols: int32 [256, 2], P(('dom', 'rep')), may hold values from 0 to 7
- link_tiles: bfloat16 [32, 128, 128], P(('dom', 'rep')), may hold values from -0.19921875 to 0.19921875
- contact_tiles: bfloat16 [512, 128, 128], P(('dom', 'rep')), may hold values from -0.29882812 to 0.29882812
- contact_owner: int32 [512, 1], P(('dom', 'rep')), may hold values from 0 to 3; in each aligned block of 16 rows (0 to 15, 16 to 31, ...) at most 8 rows name the same one
- contact_anode: int32 [512], P(('dom', 'rep')), may hold values from 0 to 7
- contact_bnode: int32 [512], P(('dom', 'rep')), may hold values from 0 to 7
Outputs:
- solution: float32 [256, 32, 128], P(('dom', 'rep'))
- residual: float32 [256, 32, 128], P(('dom', 'rep'))
Inputs may be any that keep to these rules, and one draw needn't show every extreme that they name: `contact_owner`: among the rows of one device no rep index is named by more than 8 rows.
All inputs are finite; a program needn't handle non-finite values.
Results may differ from a plain program's by a relative error of at most 0.03.
Values may be sent and summed in bfloat16 or wider, within the bound.
No kernel may reach another device: no remote copies, remote signals or barrier semaphores. Data moves between devices by JAX's collectives and lax.ppermute only.
A program may use at most 64 MiB of HBM per device.

v0:
```python
import jax
import jax.numpy as jnp
from jax import lax
from jax.sharding import PartitionSpec as P

B = 128
ITERS = 4
CAP = 8


def from_behind(value, axis, steps):
    count = lax.axis_size(axis)
    pairs = [(source, (source + steps) % count) for source in range(count)]
    return lax.ppermute(value, axis, pairs)


def partner(value, axis, distance):
    return lax.ppermute(value, axis, [(i, i ^ 1 << distance) for i in range(lax.axis_size(axis))])


def local_stiffness(rounded, diag_tiles, off_tiles, off_cols):
    nodes = rounded.shape[0]
    result = jnp.einsum("nrk,nkj->nrj", rounded, diag_tiles, preferred_element_type=jnp.float32)
    picked = rounded[off_cols]
    result = result + jnp.einsum(
        "nmrk,nmkj->nrj", picked, off_tiles, preferred_element_type=jnp.float32
    )
    mirror = jnp.einsum("nrk,nmjk->nmrj", rounded, off_tiles, preferred_element_type=jnp.float32)
    flat_cols = off_cols.reshape(-1)
    onehot = (flat_cols[:, None] == jnp.arange(nodes, dtype=jnp.int32)[None, :]).astype(jnp.float32)
    mirror = mirror.reshape(flat_cols.shape[0], rounded.shape[1], rounded.shape[2])
    return result + jnp.einsum("pn,prj->nrj", onehot, mirror, precision=lax.Precision.HIGHEST)


def contact_pairs(vector, other, near_index, far_index, contact_set):
    difference = (vector[near_index] - other[far_index]).astype(jnp.bfloat16)
    multiplier = jnp.einsum(
        "srk,skj->srj", difference, contact_set, preferred_element_type=jnp.float32
    ).astype(jnp.bfloat16)
    return jnp.einsum("srj,skj->srk", multiplier, contact_set, preferred_element_type=jnp.float32)


def collect(values, index, nodes):
    onehot = (index[:, None] == jnp.arange(nodes, dtype=jnp.int32)[None, :]).astype(jnp.float32)
    return jnp.einsum("sn,srk->nrk", onehot, values, precision=lax.Precision.HIGHEST)


def apply_operator(
    vector, diag_tiles, off_tiles, off_cols, link_tile, contact_set, near_index, far_index
):
    nodes = vector.shape[0]
    rounded = vector.astype(jnp.bfloat16)
    result = local_stiffness(rounded, diag_tiles, off_tiles, off_cols)
    before = from_behind(rounded[nodes - 1], "rep", 1)
    first_add = jnp.dot(before, link_tile, preferred_element_type=jnp.float32)
    back_term = lax.dot_general(
        rounded[0], link_tile, (((1,), (1,)), ((), ())), preferred_element_type=jnp.float32
    )
    after = from_behind(back_term, "rep", -1)
    result = result.at[0].add(first_add)
    result = result.at[nodes - 1].add(after)
    other = partner(vector.astype(jnp.bfloat16), "dom", 0).astype(vector.dtype)
    terms = contact_pairs(vector, other, near_index, far_index, contact_set)
    result = result + collect(terms, near_index, nodes)
    far_terms = partner(collect(terms, far_index, nodes).astype(jnp.bfloat16), "dom", 0).astype(
        jnp.float32
    )
    result = result - far_terms
    return result


def body(
    rhs,
    precond,
    diag_tiles,
    off_tiles,
    off_cols,
    link_tiles,
    contact_tiles,
    contact_owner,
    contact_anode,
    contact_bnode,
):
    groups = lax.axis_size("rep")
    target = contact_owner[:, 0]
    choose = (target[:, None] == jnp.arange(groups, dtype=jnp.int32)[None, :]).astype(jnp.int32)
    rank = jnp.sum((jnp.cumsum(choose, axis=0) - choose) * choose, axis=1)
    send_set = jnp.zeros((groups, CAP, B, B), jnp.bfloat16).at[target, rank].set(contact_tiles)
    labels = jnp.stack([contact_anode, contact_bnode], axis=1)
    send_labels = jnp.zeros((groups, CAP, 2), jnp.int32).at[target, rank].set(labels)
    got_set, got_labels = (
        lax.all_to_all(send_set, "rep", split_axis=0, concat_axis=0, tiled=True),
        lax.all_to_all(send_labels, "rep", split_axis=0, concat_axis=0, tiled=True),
    )
    slots = groups * CAP
    contact_set = got_set.reshape(slots, B, B)
    got_labels = got_labels.reshape(slots, 2)
    near_index = got_labels[:, 0]
    far_index = got_labels[:, 1]
    link_tile = link_tiles[0]
    scale = precond[:, None, :]
    solution = jnp.zeros_like(rhs)
    residual = rhs
    preconditioned = scale * residual
    direction = preconditioned
    res_dot = lax.psum(jnp.sum(residual * preconditioned, axis=(0, 2)), ("dom", "rep"))
    for step in range(ITERS):
        image = apply_operator(
            direction,
            diag_tiles,
            off_tiles,
            off_cols,
            link_tile,
            contact_set,
            near_index,
            far_index,
        )
        curve = lax.psum(jnp.sum(direction * image, axis=(0, 2)), ("dom", "rep"))
        alpha = res_dot / curve
        solution = solution + alpha[None, :, None] * direction
        residual = residual - alpha[None, :, None] * image
        preconditioned = scale * residual
        next_dot = lax.psum(jnp.sum(residual * preconditioned, axis=(0, 2)), ("dom", "rep"))
        direction = preconditioned + (next_dot / res_dot)[None, :, None] * direction
        res_dot = next_dot
    return (solution, residual)


def solution(mesh):
    in_specs = (
        P(("dom", "rep"), None, None),
        P(("dom", "rep"), None),
        P(("dom", "rep"), None, None),
        P(("dom", "rep"), None, None, None),
        P(("dom", "rep"), None),
        P(("dom", "rep"), None, None),
        P(("dom", "rep"), None, None),
        P(("dom", "rep"), None),
        P(("dom", "rep")),
        P(("dom", "rep")),
    )
    out_specs = (P(("dom", "rep"), None, None), P(("dom", "rep"), None, None))
    return jax.shard_map(body, mesh=mesh, in_specs=in_specs, out_specs=out_specs, check_vma=False)
```

profile of v0, /device:TPU:0, one launch (start us, length us, event | category | flops | bytes accessed | tf_op | source)
XLA Modules:
  0.0 372.2 jit_solution(10462506235294913822)
XLA Ops:
  2.4 1.3 scatter_fusion
  4.4 4.2 %all-to-all-start = ((s32[4,8,2]{1,2,0:T(2,128)}), s32[4,8,2]{1,2,0:T(2,128)S(1)}, u32[]{:S(2)}, u32[]{:S(2)}) async-start(s32[4,8,2]{1,2,0:T(2,128)} %copy.71), calls=%async_computation | async-start | bytes 8192 | tf_op jit(solution)/shard_map/all_to_all | solution.py:93
  8.7 2.1 collective-permute-start.2
  11.1 1.6 collective-permute-start.1
  15.9 2.8 scatter_fusion.1
  18.7 3.5 all-to-all-start.1
  23.1 1.4 gather_fusion.2
  24.5 12.1 %all-to-all-done.1 = bf16[4,8,128,128]{3,2,1,0:T(8,128)(2,1)S(1)} async-done(((bf16[4,8,128,128]{3,2,1,0:T(8,128)(2,1)}), bf16[4,8,128,128]{3,2,1,0:T(8,128)(2,1)S(1)}, u32[]{:S(2)}, u32[]{:S(2)}) %all-to-all-start.1) | async-done | bytes 1048608 | tf_op jit(solution)/shard_map/all_to_all | solution.py:92
  36.6 2.0 fusion
  40.5 3.1 collective-permute-done.3
  43.7 39.5 %all-reduce = (f32[32]{0:T(128)S(1)}, f32[32]{0:T(128)S(1)}) all-reduce(f32[32]{0:T(128)S(1)} %get-tuple-element.99, f32[32]{0:T(128)S(1)} %get-tuple-element.98), channel_id=1, replica_groups=mesh['dom'=8,'rep'=4] {'dom','rep'}, use_global_device_ids=true, to_apply=%region_1.2 | all-reduce | flops 64 | bytes 512 | tf_op jit(solution)/shard_map/psum | solution.py:106
  83.4 40.3 %psum.58 = f32[32]{0:T(128)S(1)} all-reduce(f32[32]{0:T(128)S(1)} %get-tuple-element.112), channel_id=1, replica_groups=mesh['dom'=8,'rep'=4] {'dom','rep'}, use_global_device_ids=true, to_apply=%region_9.10 | all-reduce | flops 32 | bytes 256 | tf_op jit(solution)/shard_map/psum | solution.py:123
  123.9 2.3 collective-permute-start.6
  129.1 1.7 collective-permute-start.5
  132.3 1.4 gather_fusion.5
  133.7 2.0 fusion.1
  136.9 4.0 %collective-permute-done.7 = bf16[8,32,128]{2,1,0:T(8,128)(2,1)S(1)} collective-permute-done((bf16[8,32,128]{2,1,0:T(8,128)(2,1)S(1)}, bf16[8,32,128]{2,1,0:T(8,128)(2,1)S(1)}, u32[]{:S(2)}, u32[]{:S(2)}) %collective-permute-start.7) | collective-permute-done | bytes 65568 | tf_op jit(solution)/shard_map/ppermute | solution.py:18
  141.1 38.3 %psum.59 = f32[32]{0:T(128)S(1)} all-reduce(f32[32]{0:T(128)S(1)} %multiply_reduce_fusion.2), channel_id=1, replica_groups=mesh['dom'=8,'rep'=4] {'dom','rep'}, use_global_device_ids=true, to_apply=%region_11.12 | all-reduce | flops 32 | bytes 256 | tf_op jit(solution)/shard_map/psum | solution.py:118
  179.5 41.1 %psum.60 = f32[32]{0:T(128)S(1)} all-reduce(f32[32]{0:T(128)S(1)} %get-tuple-element.108), channel_id=1, replica_groups=mesh['dom'=8,'rep'=4] {'dom','rep'}, use_global_device_ids=true, to_apply=%region_13.14 | all-reduce | flops 32 | bytes 256 | tf_op jit(solution)/shard_map/psum | solution.py:123
  220.7 2.3 collective-permute-start.10
  226.1 1.7 collective-permute-start.9
  229.3 1.4 gather_fusion.8
  230.7 2.0 fusion.2
  234.0 3.9 %collective-permute-done.11 = bf16[8,32,128]{2,1,0:T(8,128)(2,1)S(1)} collective-permute-done((bf16[8,32,128]{2,1,0:T(8,128)(2,1)S(1)}, bf16[8,32,128]{2,1,0:T(8,128)(2,1)S(1)}, u32[]{:S(2)}, u32[]{:S(2)}) %collective-permute-start.11) | collective-permute-done | bytes 65568 | tf_op jit(solution)/shard_map/ppermute | solution.py:18
  238.0 38.3 %psum.61 = f32[32]{0:T(128)S(1)} all-reduce(f32[32]{0:T(128)S(1)} %multiply_reduce_fusion.1), channel_id=1, replica_groups=mesh['dom'=8,'rep'=4] {'dom','rep'}, use_global_device_ids=true, to_apply=%region_15.16 | all-reduce | flops 32 | bytes 256 | tf_op jit(solution)/shard_map/psum | solution.py:118
  276.6 39.8 %psum.62 = f32[32]{0:T(128)S(1)} all-reduce(f32[32]{0:T(128)S(1)} %get-tuple-element.104), channel_id=1, replica_groups=mesh['dom'=8,'rep'=4] {'dom','rep'}, use_global_device_ids=true, to_apply=%region_17.18 | all-reduce | flops 32 | bytes 256 | tf_op jit(solution)/shard_map/psum | solution.py:123
  316.5 2.3 collective-permute-start.14
  321.1 1.7 collective-permute-start.13
  324.3 1.4 gather_fusion.11
  325.7 2.0 fusion.3
  328.9 3.7 collective-permute-done.15
  332.7 38.6 %psum.63 = f32[32]{0:T(128)S(1)} all-reduce(f32[32]{0:T(128)S(1)} %multiply_reduce_fusion), channel_id=1, replica_groups=mesh['dom'=8,'rep'=4] {'dom','rep'}, use_global_device_ids=true, to_apply=%region_19.20 | all-reduce | flops 32 | bytes 256 | tf_op jit(solution)/shard_map/psum | solution.py:118
  (143 shorter events, 27.3 us)
Async XLA Ops:
  0.6 13.1 %copy-start = (bf16[8,2,128,128]{3,2,1,0:T(8,128)(2,1)S(1)}, bf16[8,2,128,128]{3,2,1,0:T(8,128)(2,1)}, u32[]{:S(2)}) copy-start(bf16[8,2,128,128]{3,2,1,0:T(8,128)(2,1)} %param.29) | copy-start | bytes 1572868
  0.6 0.7 copy-start.13
  0.7 8.0 %copy-start.2 = (f32[8,32,128]{2,1,0:T(8,128)S(1)}, f32[8,32,128]{2,1,0:T(8,128)}, u32[]{:S(2)}) copy-start(f32[8,32,128]{2,1,0:T(8,128)} %param.26) | copy-start | bytes 393220
  2.4 6.2 %copy-start.11 = (f32[8,128]{1,0:T(8,128)S(1)}, f32[8,128]{1,0:T(8,128)}, u32[]{:S(2)}) copy-start(f32[8,128]{1,0:T(8,128)} %param.27) | copy-start | bytes 12292
  2.4 10.4 %copy-start.1 = (bf16[8,128,128]{2,1,0:T(8,128)(2,1)S(1)}, bf16[8,128,128]{2,1,0:T(8,128)(2,1)}, u32[]{:S(2)}) copy-start(bf16[8,128,128]{2,1,0:T(8,128)(2,1)} %param.28) | copy-start | bytes 786436
  4.4 14.2 %all-to-all-start = ((s32[4,8,2]{1,2,0:T(2,128)}), s32[4,8,2]{1,2,0:T(2,128)S(1)}, u32[]{:S(2)}, u32[]{:S(2)}) async-start(s32[4,8,2]{1,2,0:T(2,128)} %copy.71), calls=%async_computation | async-start | bytes 8192 | tf_op jit(solution)/shard_map/all_to_all | solution.py:93
  8.7 2.3 copy-start.3
  8.7 14.4 %collective-permute-start.2 = (bf16[8,32,128]{2,1,0:T(8,128)(2,1)S(1)}, bf16[8,32,128]{2,1,0:T(8,128)(2,1)S(1)}, u32[]{:S(2)}, u32[]{:S(2)}) collective-permute-start(bf16[8,32,128]{2,1,0:T(8,128)(2,1)S(1)} %get-tuple-element.114), channel_id=1, source_target_pairs={{0,4},{4,0},{8,12},{12,8},{16,20},{20,16},{24,28},{28,24},{1,5},{5... | collective-permute-start | bytes 196616 | tf_op jit(solution)/shard_map/ppermute | solution.py:18
  10.8 1.9 copy-start.12
  10.8 12.1 %collective-permute-start = (bf16[32,128]{1,0:T(8,128)(2,1)S(1)}, bf16[32,128]{1,0:T(8,128)(2,1)S(1)}, u32[]{:S(2)}, u32[]{:S(2)}) collective-permute-start(bf16[32,128]{1,0:T(8,128)(2,1)S(1)} %slice_bitcast_fusion.11), channel_id=1, source_target_pairs={{0,1},{1,2},{2,3},{3,0},{4,5},{5,6},{6,7},{7,4},{8,9},{9,10},{10,1... | collective-permute-start | bytes 24584 | tf_op jit(solution)/shard_map/ppermute | solution.py:14
  11.1 12.0 %collective-permute-start.1 = (f32[32,128]{1,0:T(8,128)S(1)}, f32[32,128]{1,0:T(8,128)S(1)}, u32[]{:S(2)}, u32[]{:S(2)}) collective-permute-start(f32[32,128]{1,0:T(8,128)S(1)} %fusion.68), channel_id=1, source_target_pairs={{0,3},{1,0},{2,1},{3,2},{4,7},{5,4},{6,5},{7,6},{8,11},{9,8},{10,9... | collective-permute-start | bytes 49160 | tf_op jit(solution)/shard_map/ppermute | solution.py:14
  14.7 1.2 copy-start.8
  18.7 18.0 %all-to-all-start.1 = ((bf16[4,8,128,128]{3,2,1,0:T(8,128)(2,1)}), bf16[4,8,128,128]{3,2,1,0:T(8,128)(2,1)S(1)}, u32[]{:S(2)}, u32[]{:S(2)}) async-start(bf16[4,8,128,128]{3,2,1,0:T(8,128)(2,1)} %scatter_fusion.1), calls=%async_computation.1 | async-start | bytes 2097152 | tf_op jit(solution)/shard_map/all_to_all | solution.py:92
  39.2 4.3 %collective-permute-start.3 = (bf16[8,32,128]{2,1,0:T(8,128)(2,1)S(1)}, bf16[8,32,128]{2,1,0:T(8,128)(2,1)S(1)}, u32[]{:S(2)}, u32[]{:S(2)}) collective-permute-start(bf16[8,32,128]{2,1,0:T(8,128)(2,1)S(1)} %copy.166), channel_id=1, source_target_pairs={{0,4},{4,0},{8,12},{12,8},{16,20},{20,16},{24,28},{28,24},{1,5},{5... | collective-permute-start | bytes 196616 | tf_op jit(solution)/shard_map/ppermute | solution.py:18
  123.9 8.4 %collective-permute-start.6 = (bf16[8,32,128]{2,1,0:T(8,128)(2,1)S(1)}, bf16[8,32,128]{2,1,0:T(8,128)(2,1)S(1)}, u32[]{:S(2)}, u32[]{:S(2)}) collective-permute-start(bf16[8,32,128]{2,1,0:T(8,128)(2,1)S(1)} %get-tuple-element.110), channel_id=1, source_target_pairs={{0,4},{4,0},{8,12},{12,8},{16,20},{20,16},{24,28},{28,24},{1,5},{5... | collective-permute-start | bytes 196616 | tf_op jit(solution)/shard_map/ppermute | solution.py:18
  128.6 2.2 copy-start.9
  129.0 3.1 collective-permute-start.4
  129.1 3.2 collective-permute-start.5
  136.3 4.6 %collective-permute-start.7 = (bf16[8,32,128]{2,1,0:T(8,128)(2,1)S(1)}, bf16[8,32,128]{2,1,0:T(8,128)(2,1)S(1)}, u32[]{:S(2)}, u32[]{:S(2)}) collective-permute-start(bf16[8,32,128]{2,1,0:T(8,128)(2,1)S(1)} %copy.165), channel_id=1, source_target_pairs={{0,4},{4,0},{8,12},{12,8},{16,20},{20,16},{24,28},{28,24},{1,5},{5... | collective-permute-start | bytes 196616 | tf_op jit(solution)/shard_map/ppermute | solution.py:18
  179.5 41.2 %copy-start.6 = (f32[8,32,128]{2,1,0:T(8,128)}, f32[8,32,128]{2,1,0:T(8,128)S(1)}, u32[]{:S(2)}) copy-start(f32[8,32,128]{2,1,0:T(8,128)S(1)} %get-tuple-element.109) | copy-start | bytes 393220
  220.7 8.6 %collective-permute-start.10 = (bf16[8,32,128]{2,1,0:T(8,128)(2,1)S(1)}, bf16[8,32,128]{2,1,0:T(8,128)(2,1)S(1)}, u32[]{:S(2)}, u32[]{:S(2)}) collective-permute-start(bf16[8,32,128]{2,1,0:T(8,128)(2,1)S(1)} %get-tuple-element.106), channel_id=1, source_target_pairs={{0,4},{4,0},{8,12},{12,8},{16,20},{20,16},{24,28},{28,24},{1,5},{5... | collective-permute-start | bytes 196616 | tf_op jit(solution)/shard_map/ppermute | solution.py:18
  225.5 2.4 copy-start.10
  225.8 3.3 collective-permute-start.8
  226.1 3.2 collective-permute-start.9
  233.3 4.6 %collective-permute-start.11 = (bf16[8,32,128]{2,1,0:T(8,128)(2,1)S(1)}, bf16[8,32,128]{2,1,0:T(8,128)(2,1)S(1)}, u32[]{:S(2)}, u32[]{:S(2)}) collective-permute-start(bf16[8,32,128]{2,1,0:T(8,128)(2,1)S(1)} %copy.164), channel_id=1, source_target_pairs={{0,4},{4,0},{8,12},{12,8},{16,20},{20,16},{24,28},{28,24},{1,5},{5... | collective-permute-start | bytes 196616 | tf_op jit(solution)/shard_map/ppermute | solution.py:18
  233.9 42.4 %copy-start.7 = (f32[8,32,128]{2,1,0:T(8,128)S(1)}, f32[8,32,128]{2,1,0:T(8,128)}, u32[]{:S(2)}) copy-start(f32[8,32,128]{2,1,0:T(8,128)} %copy-done.6) | copy-start | bytes 393220
  276.6 39.9 %copy-start.4 = (f32[8,32,128]{2,1,0:T(8,128)}, f32[8,32,128]{2,1,0:T(8,128)S(1)}, u32[]{:S(2)}) copy-start(f32[8,32,128]{2,1,0:T(8,128)S(1)} %get-tuple-element.105) | copy-start | bytes 393220
  316.5 7.8 %collective-permute-start.14 = (bf16[8,32,128]{2,1,0:T(8,128)(2,1)S(1)}, bf16[8,32,128]{2,1,0:T(8,128)(2,1)S(1)}, u32[]{:S(2)}, u32[]{:S(2)}) collective-permute-start(bf16[8,32,128]{2,1,0:T(8,128)(2,1)S(1)} %get-tuple-element.102), channel_id=1, source_target_pairs={{0,4},{4,0},{8,12},{12,8},{16,20},{20,16},{24,28},{28,24},{1,5},{5... | collective-permute-start | bytes 196616 | tf_op jit(solution)/shard_map/ppermute | solution.py:18
  321.0 3.1 collective-permute-start.12
  321.1 3.2 collective-permute-start.13
  328.3 4.3 %collective-permute-start.15 = (bf16[8,32,128]{2,1,0:T(8,128)(2,1)S(1)}, bf16[8,32,128]{2,1,0:T(8,128)(2,1)S(1)}, u32[]{:S(2)}, u32[]{:S(2)}) collective-permute-start(bf16[8,32,128]{2,1,0:T(8,128)(2,1)S(1)} %copy.163), channel_id=1, source_target_pairs={{0,4},{4,0},{8,12},{12,8},{16,20},{20,16},{24,28},{28,24},{1,5},{5... | collective-permute-start | bytes 196616 | tf_op jit(solution)/shard_map/ppermute | solution.py:18
  328.9 42.5 %copy-start.5 = (f32[8,32,128]{2,1,0:T(8,128)S(1)}, f32[8,32,128]{2,1,0:T(8,128)}, u32[]{:S(2)}) copy-start(f32[8,32,128]{2,1,0:T(8,128)} %copy-done.4) | copy-start | bytes 393220
where the time goes:
time: 373 us; the launch traced here: 372 us
  blocking collectives  276 us (74%)
  waiting for transfers between devices  30.1 us (8%)
  starting transfers between devices  25.1 us (7%)
  local copies, waits for them, and re-layouts  18.9 us (5%)
  matrix products  17.6 us (5%)
    psum x4, blocking collectives, body(): lax.psum(jnp.sum(residual * preconditioned, axis=(0, 2)), ('dom', 'rep'))  161 us
    psum x3, blocking collectives, body(): curve = lax.psum(jnp.sum(direction * image, axis=(0, 2)), ('dom', 'rep'))  115 us
    ppermute x8, waiting for transfers between devices, partner(): lax.ppermute(value, axis, [(i, i ^ 1 << distance) for i in range(lax.axis...  14.6 us
    all_to_all x1, waiting for transfers between devices, body(): lax.all_to_all(send_set, 'rep', split_axis=0, concat_axis=0, tiled=True)  12.1 us
    ppermute x8, starting transfers between devices, partner(): lax.ppermute(value, axis, [(i, i ^ 1 << distance) for i in range(lax.axis...  10 us
    gather x8, local copies, waits for them, and re-layouts, contact_pairs(): difference = (vector[near_index] - other[far_index]).astype(jnp.bfloat16)  7.96 us
    dot_general x4, matrix products, contact_pairs(): jnp.einsum('srj,skj->srk', multiplier, contact_set, preferred_element_typ...  7.84 us
  transfers between devices with their start and end apart: 18, of which 8 were waited for; matrix products, arithmetic and copies ran while one was open for 5% of the time, Pallas kernels for 0%

commit v1 on v0

--- a/solution.py
+++ b/solution.py
@@ -120,7 +120,8 @@
         solution = solution + alpha[None, :, None] * direction
         residual = residual - alpha[None, :, None] * image
         preconditioned = scale * residual
-        next_dot = lax.psum(jnp.sum(residual * preconditioned, axis=(0, 2)), ("dom", "rep"))
+        one_axis = lax.psum(jnp.sum(residual * preconditioned, axis=(0, 2)), "rep")
+        next_dot = lax.psum(one_axis, "dom")
         direction = preconditioned + (next_dot / res_dot)[None, :, None] * direction
         res_dot = next_dot
     return (solution, residual)

time: 373 us -> 324 us (0.87)
  blocking collectives: 276 us -> 233 us
  waiting for transfers between devices: 30.1 us -> 24.5 us
    psum x4 -> x1, blocking collectives: 161 us -> 39.5 us  [body(): lax.psum(jnp.sum(residual * preconditioned, axis=(0, 2)), ('dom', 'rep'))]
    psum x0 -> x6, blocking collectives: none -> 80.4 us  [the longest x3 62.1 us: body(): next_dot = lax.psum(one_axis, 'dom')]
    ppermute x8, waiting for transfers between devices: 14.6 us -> 9.05 us  [partner(): lax.ppermute(value, axis, [(i, i ^ 1 << distance) for i in range(lax.axis...]
  transfers between devices with their start and end apart: 18 -> 18, of which waited for: 8 -> 8; matrix products, arithmetic and copies ran while one was open for 5% -> 6% of each run, Pallas kernels for 0% -> 0%
where the time goes in v1:
time: 324 us; the launch traced here: 322 us
  blocking collectives  233 us (72%)
  waiting for transfers between devices  24.5 us (8%)
  starting transfers between devices  24.1 us (7%)
  local copies, waits for them, and re-layouts  18.9 us (6%)
  matrix products  17.6 us (5%)
  other arithmetic  3.45 us (1%)
    psum x3, blocking collectives, body(): curve = lax.psum(jnp.sum(direction * image, axis=(0, 2)), ('dom', 'rep'))  113 us
    psum x3, blocking collectives, body(): next_dot = lax.psum(one_axis, 'dom')  62.1 us
    psum x1, blocking collectives, body(): lax.psum(jnp.sum(residual * preconditioned, axis=(0, 2)), ('dom', 'rep'))  39.5 us
    psum x3, blocking collectives, body(): one_axis = lax.psum(jnp.sum(residual * preconditioned, axis=(0, 2)), 'rep')  18.3 us
    all_to_all x1, waiting for transfers between devices, body(): lax.all_to_all(send_set, 'rep', split_axis=0, concat_axis=0, tiled=True)  12.1 us
    ppermute x8, starting transfers between devices, partner(): lax.ppermute(value, axis, [(i, i ^ 1 << distance) for i in range(lax.axis...  9.24 us
    ppermute x8, waiting for transfers between devices, partner(): lax.ppermute(value, axis, [(i, i ^ 1 << distance) for i in range(lax.axis...  9.05 us
    gather x8, local copies, waits for them, and re-layouts, contact_pairs(): difference = (vector[near_index] - other[far_index]).astype(jnp.bfloat16)  7.96 us
  transfers between devices with their start and end apart: 18, of which 8 were waited for; matrix products, arithmetic and copies ran while one was open for 6% of the time, Pallas kernels for 0%

profile of v1, /device:TPU:0, one launch (start us, length us, event | category | flops | bytes accessed | tf_op | source)
XLA Modules:
  0.0 322.4 jit_solution(1336385359122607985)
XLA Ops:
  4.4 4.2 %all-to-all-start = ((s32[4,8,2]{1,2,0:T(2,128)}), s32[4,8,2]{1,2,0:T(2,128)S(1)}, u32[]{:S(2)}, u32[]{:S(2)}) async-start(s32[4,8,2]{1,2,0:T(2,128)} %copy.71), calls=%async_computation | async-start | bytes 8192 | tf_op jit(solution)/shard_map/all_to_all | solution.py:93
  8.7 2.1 collective-permute-start.2
  11.1 1.6 collective-permute-start.1
  15.9 2.8 scatter_fusion.1
  18.7 3.5 %all-to-all-start.1 = ((bf16[4,8,128,128]{3,2,1,0:T(8,128)(2,1)}), bf16[4,8,128,128]{3,2,1,0:T(8,128)(2,1)S(1)}, u32[]{:S(2)}, u32[]{:S(2)}) async-start(bf16[4,8,128,128]{3,2,1,0:T(8,128)(2,1)} %scatter_fusion.1), calls=%async_computation.1 | async-start | bytes 2097152 | tf_op jit(solution)/shard_map/all_to_all | solution.py:92
  23.1 1.4 gather_fusion.2
  24.5 12.1 %all-to-all-done.1 = bf16[4,8,128,128]{3,2,1,0:T(8,128)(2,1)S(1)} async-done(((bf16[4,8,128,128]{3,2,1,0:T(8,128)(2,1)}), bf16[4,8,128,128]{3,2,1,0:T(8,128)(2,1)S(1)}, u32[]{:S(2)}, u32[]{:S(2)}) %all-to-all-start.1) | async-done | bytes 1048608 | tf_op jit(solution)/shard_map/all_to_all | solution.py:92
  36.6 2.0 fusion
  40.5 3.1 collective-permute-done.3
  43.7 39.5 %all-reduce = (f32[32]{0:T(128)S(1)}, f32[32]{0:T(128)S(1)}) all-reduce(f32[32]{0:T(128)S(1)} %get-tuple-element.99, f32[32]{0:T(128)S(1)} %get-tuple-element.98), channel_id=1, replica_groups=mesh['dom'=8,'rep'=4] {'dom','rep'}, use_global_device_ids=true, to_apply=%region_1.2 | all-reduce | flops 64 | bytes 512 | tf_op jit(solution)/shard_map/psum | solution.py:106
  83.4 5.8 %psum.79 = f32[32]{0:T(128)S(1)} all-reduce(f32[32]{0:T(128)S(1)} %get-tuple-element.112), channel_id=1, replica_groups=mesh['dom'=8,'rep'=4] {'rep'}, use_global_device_ids=true, to_apply=%region_9.10 | all-reduce | flops 32 | bytes 256 | tf_op jit(solution)/shard_map/psum | solution.py:123
  89.3 20.9 %psum.80 = f32[32]{0:T(128)S(1)} all-reduce(f32[32]{0:T(128)S(1)} %psum.79), channel_id=1, replica_groups=mesh['dom'=8,'rep'=4] {'dom'}, use_global_device_ids=true, to_apply=%region_10.11 | all-reduce | flops 32 | bytes 256 | tf_op jit(solution)/shard_map/psum | solution.py:124
  113.2 1.7 collective-permute-start.5
  116.5 1.4 gather_fusion.5
  117.9 2.0 fusion.1
  120.4 2.1 collective-permute-start.7
  123.1 2.4 collective-permute-done.7
  125.6 37.1 %psum.81 = f32[32]{0:T(128)S(1)} all-reduce(f32[32]{0:T(128)S(1)} %multiply_reduce_fusion.2), channel_id=1, replica_groups=mesh['dom'=8,'rep'=4] {'dom','rep'}, use_global_device_ids=true, to_apply=%region_12.13 | all-reduce | flops 32 | bytes 256 | tf_op jit(solution)/shard_map/psum | solution.py:118
  163.0 6.6 %psum.82 = f32[32]{0:T(128)S(1)} all-reduce(f32[32]{0:T(128)S(1)} %get-tuple-element.108), channel_id=1, replica_groups=mesh['dom'=8,'rep'=4] {'rep'}, use_global_device_ids=true, to_apply=%region_14.15 | all-reduce | flops 32 | bytes 256 | tf_op jit(solution)/shard_map/psum | solution.py:123
  169.6 20.1 %psum.83 = f32[32]{0:T(128)S(1)} all-reduce(f32[32]{0:T(128)S(1)} %psum.82), channel_id=1, replica_groups=mesh['dom'=8,'rep'=4] {'dom'}, use_global_device_ids=true, to_apply=%region_15.16 | all-reduce | flops 32 | bytes 256 | tf_op jit(solution)/shard_map/psum | solution.py:124
  192.8 1.8 collective-permute-start.9
  197.4 2.0 fusion.2
  200.0 2.1 collective-permute-start.11
  202.7 1.7 collective-permute-done.11
  204.5 38.7 %psum.84 = f32[32]{0:T(128)S(1)} all-reduce(f32[32]{0:T(128)S(1)} %multiply_reduce_fusion.1), channel_id=1, replica_groups=mesh['dom'=8,'rep'=4] {'dom','rep'}, use_global_device_ids=true, to_apply=%region_17.18 | all-reduce | flops 32 | bytes 256 | tf_op jit(solution)/shard_map/psum | solution.py:118
  243.4 5.8 %psum.85 = f32[32]{0:T(128)S(1)} all-reduce(f32[32]{0:T(128)S(1)} %get-tuple-element.104), channel_id=1, replica_groups=mesh['dom'=8,'rep'=4] {'rep'}, use_global_device_ids=true, to_apply=%region_19.20 | all-reduce | flops 32 | bytes 256 | tf_op jit(solution)/shard_map/psum | solution.py:123
  249.2 21.0 %psum.86 = f32[32]{0:T(128)S(1)} all-reduce(f32[32]{0:T(128)S(1)} %psum.85), channel_id=1, replica_groups=mesh['dom'=8,'rep'=4] {'dom'}, use_global_device_ids=true, to_apply=%region_20.21 | all-reduce | flops 32 | bytes 256 | tf_op jit(solution)/shard_map/psum | solution.py:124
  272.7 1.7 collective-permute-start.13
  277.3 2.0 fusion.3
  279.9 2.1 collective-permute-start.15
  282.6 2.0 collective-permute-done.15
  284.7 36.9 %psum.87 = f32[32]{0:T(128)S(1)} all-reduce(f32[32]{0:T(128)S(1)} %multiply_reduce_fusion), channel_id=1, replica_groups=mesh['dom'=8,'rep'=4] {'dom','rep'}, use_global_device_ids=true, to_apply=%region_22.23 | all-reduce | flops 32 | bytes 256 | tf_op jit(solution)/shard_map/psum | solution.py:118
  (146 shorter events, 31.1 us)
Async XLA Ops:
  0.6 13.1 %copy-start = (bf16[8,2,128,128]{3,2,1,0:T(8,128)(2,1)S(1)}, bf16[8,2,128,128]{3,2,1,0:T(8,128)(2,1)}, u32[]{:S(2)}) copy-start(bf16[8,2,128,128]{3,2,1,0:T(8,128)(2,1)} %param.29) | copy-start | bytes 1572868
  0.6 0.7 copy-start.13
  0.7 8.0 %copy-start.2 = (f32[8,32,128]{2,1,0:T(8,128)S(1)}, f32[8,32,128]{2,1,0:T(8,128)}, u32[]{:S(2)}) copy-start(f32[8,32,128]{2,1,0:T(8,128)} %param.26) | copy-start | bytes 393220
  2.4 6.2 %copy-start.11 = (f32[8,128]{1,0:T(8,128)S(1)}, f32[8,128]{1,0:T(8,128)}, u32[]{:S(2)}) copy-start(f32[8,128]{1,0:T(8,128)} %param.27) | copy-start | bytes 12292
  2.4 10.4 %copy-start.1 = (bf16[8,128,128]{2,1,0:T(8,128)(2,1)S(1)}, bf16[8,128,128]{2,1,0:T(8,128)(2,1)}, u32[]{:S(2)}) copy-start(bf16[8,128,128]{2,1,0:T(8,128)(2,1)} %param.28) | copy-start | bytes 786436
  4.4 14.2 %all-to-all-start = ((s32[4,8,2]{1,2,0:T(2,128)}), s32[4,8,2]{1,2,0:T(2,128)S(1)}, u32[]{:S(2)}, u32[]{:S(2)}) async-start(s32[4,8,2]{1,2,0:T(2,128)} %copy.71), calls=%async_computation | async-start | bytes 8192 | tf_op jit(solution)/shard_map/all_to_all | solution.py:93
  8.7 2.3 copy-start.3
  8.7 14.4 %collective-permute-start.2 = (bf16[8,32,128]{2,1,0:T(8,128)(2,1)S(1)}, bf16[8,32,128]{2,1,0:T(8,128)(2,1)S(1)}, u32[]{:S(2)}, u32[]{:S(2)}) collective-permute-start(bf16[8,32,128]{2,1,0:T(8,128)(2,1)S(1)} %get-tuple-element.114), channel_id=1, source_target_pairs={{0,4},{4,0},{8,12},{12,8},{16,20},{20,16},{24,28},{28,24},{1,5},{5... | collective-permute-start | bytes 196616 | tf_op jit(solution)/shard_map/ppermute | solution.py:18
  10.8 1.9 copy-start.12
  10.8 12.1 %collective-permute-start = (bf16[32,128]{1,0:T(8,128)(2,1)S(1)}, bf16[32,128]{1,0:T(8,128)(2,1)S(1)}, u32[]{:S(2)}, u32[]{:S(2)}) collective-permute-start(bf16[32,128]{1,0:T(8,128)(2,1)S(1)} %slice_bitcast_fusion.11), channel_id=1, source_target_pairs={{0,1},{1,2},{2,3},{3,0},{4,5},{5,6},{6,7},{7,4},{8,9},{9,10},{10,1... | collective-permute-start | bytes 24584 | tf_op jit(solution)/shard_map/ppermute | solution.py:14
  11.1 12.0 %collective-permute-start.1 = (f32[32,128]{1,0:T(8,128)S(1)}, f32[32,128]{1,0:T(8,128)S(1)}, u32[]{:S(2)}, u32[]{:S(2)}) collective-permute-start(f32[32,128]{1,0:T(8,128)S(1)} %fusion.68), channel_id=1, source_target_pairs={{0,3},{1,0},{2,1},{3,2},{4,7},{5,4},{6,5},{7,6},{8,11},{9,8},{10,9... | collective-permute-start | bytes 49160 | tf_op jit(solution)/shard_map/ppermute | solution.py:14
  14.7 1.2 copy-start.8
  18.7 18.0 %all-to-all-start.1 = ((bf16[4,8,128,128]{3,2,1,0:T(8,128)(2,1)}), bf16[4,8,128,128]{3,2,1,0:T(8,128)(2,1)S(1)}, u32[]{:S(2)}, u32[]{:S(2)}) async-start(bf16[4,8,128,128]{3,2,1,0:T(8,128)(2,1)} %scatter_fusion.1), calls=%async_computation.1 | async-start | bytes 2097152 | tf_op jit(solution)/shard_map/all_to_all | solution.py:92
  39.2 4.3 %collective-permute-start.3 = (bf16[8,32,128]{2,1,0:T(8,128)(2,1)S(1)}, bf16[8,32,128]{2,1,0:T(8,128)(2,1)S(1)}, u32[]{:S(2)}, u32[]{:S(2)}) collective-permute-start(bf16[8,32,128]{2,1,0:T(8,128)(2,1)S(1)} %copy.166), channel_id=1, source_target_pairs={{0,4},{4,0},{8,12},{12,8},{16,20},{20,16},{24,28},{28,24},{1,5},{5... | collective-permute-start | bytes 196616 | tf_op jit(solution)/shard_map/ppermute | solution.py:18
  110.3 6.2 %collective-permute-start.6 = (bf16[8,32,128]{2,1,0:T(8,128)(2,1)S(1)}, bf16[8,32,128]{2,1,0:T(8,128)(2,1)S(1)}, u32[]{:S(2)}, u32[]{:S(2)}) collective-permute-start(bf16[8,32,128]{2,1,0:T(8,128)(2,1)S(1)} %get-tuple-element.110), channel_id=1, source_target_pairs={{0,4},{4,0},{8,12},{12,8},{16,20},{20,16},{24,28},{28,24},{1,5},{5... | collective-permute-start | bytes 196616 | tf_op jit(solution)/shard_map/ppermute | solution.py:18
  112.8 2.2 copy-start.9
  113.2 3.1 collective-permute-start.4
  113.2 3.2 collective-permute-start.5
  120.4 5.0 %collective-permute-start.7 = (bf16[8,32,128]{2,1,0:T(8,128)(2,1)S(1)}, bf16[8,32,128]{2,1,0:T(8,128)(2,1)S(1)}, u32[]{:S(2)}, u32[]{:S(2)}) collective-permute-start(bf16[8,32,128]{2,1,0:T(8,128)(2,1)S(1)} %copy.165), channel_id=1, source_target_pairs={{0,4},{4,0},{8,12},{12,8},{16,20},{20,16},{24,28},{28,24},{1,5},{5... | collective-permute-start | bytes 196616 | tf_op jit(solution)/shard_map/ppermute | solution.py:18
  163.0 26.9 %copy-start.6 = (f32[8,32,128]{2,1,0:T(8,128)}, f32[8,32,128]{2,1,0:T(8,128)S(1)}, u32[]{:S(2)}) copy-start(f32[8,32,128]{2,1,0:T(8,128)S(1)} %get-tuple-element.109) | copy-start | bytes 393220
  189.8 6.2 %collective-permute-start.10 = (bf16[8,32,128]{2,1,0:T(8,128)(2,1)S(1)}, bf16[8,32,128]{2,1,0:T(8,128)(2,1)S(1)}, u32[]{:S(2)}, u32[]{:S(2)}) collective-permute-start(bf16[8,32,128]{2,1,0:T(8,128)(2,1)S(1)} %get-tuple-element.106), channel_id=1, source_target_pairs={{0,4},{4,0},{8,12},{12,8},{16,20},{20,16},{24,28},{28,24},{1,5},{5... | collective-permute-start | bytes 196616 | tf_op jit(solution)/shard_map/ppermute | solution.py:18
  192.3 2.2 copy-start.10
  192.7 3.1 collective-permute-start.8
  192.8 3.2 collective-permute-start.9
  200.0 4.3 %collective-permute-start.11 = (bf16[8,32,128]{2,1,0:T(8,128)(2,1)S(1)}, bf16[8,32,128]{2,1,0:T(8,128)(2,1)S(1)}, u32[]{:S(2)}, u32[]{:S(2)}) collective-permute-start(bf16[8,32,128]{2,1,0:T(8,128)(2,1)S(1)} %copy.164), channel_id=1, source_target_pairs={{0,4},{4,0},{8,12},{12,8},{16,20},{20,16},{24,28},{28,24},{1,5},{5... | collective-permute-start | bytes 196616 | tf_op jit(solution)/shard_map/ppermute | solution.py:18
  202.6 40.5 %copy-start.7 = (f32[8,32,128]{2,1,0:T(8,128)S(1)}, f32[8,32,128]{2,1,0:T(8,128)}, u32[]{:S(2)}) copy-start(f32[8,32,128]{2,1,0:T(8,128)} %copy-done.6) | copy-start | bytes 393220
  243.4 27.0 %copy-start.4 = (f32[8,32,128]{2,1,0:T(8,128)}, f32[8,32,128]{2,1,0:T(8,128)S(1)}, u32[]{:S(2)}) copy-start(f32[8,32,128]{2,1,0:T(8,128)S(1)} %get-tuple-element.105) | copy-start | bytes 393220
  270.4 5.5 %collective-permute-start.14 = (bf16[8,32,128]{2,1,0:T(8,128)(2,1)S(1)}, bf16[8,32,128]{2,1,0:T(8,128)(2,1)S(1)}, u32[]{:S(2)}, u32[]{:S(2)}) collective-permute-start(bf16[8,32,128]{2,1,0:T(8,128)(2,1)S(1)} %get-tuple-element.102), channel_id=1, source_target_pairs={{0,4},{4,0},{8,12},{12,8},{16,20},{20,16},{24,28},{28,24},{1,5},{5... | collective-permute-start | bytes 196616 | tf_op jit(solution)/shard_map/ppermute | solution.py:18
  272.6 3.1 collective-permute-start.12
  272.7 3.2 collective-permute-start.13
  279.9 4.6 %collective-permute-start.15 = (bf16[8,32,128]{2,1,0:T(8,128)(2,1)S(1)}, bf16[8,32,128]{2,1,0:T(8,128)(2,1)S(1)}, u32[]{:S(2)}, u32[]{:S(2)}) collective-permute-start(bf16[8,32,128]{2,1,0:T(8,128)(2,1)S(1)} %copy.163), channel_id=1, source_target_pairs={{0,4},{4,0},{8,12},{12,8},{16,20},{20,16},{24,28},{28,24},{1,5},{5... | collective-permute-start | bytes 196616 | tf_op jit(solution)/shard_map/ppermute | solution.py:18
  282.6 39.1 %copy-start.5 = (f32[8,32,128]{2,1,0:T(8,128)S(1)}, f32[8,32,128]{2,1,0:T(8,128)}, u32[]{:S(2)}) copy-start(f32[8,32,128]{2,1,0:T(8,128)} %copy-done.4) | copy-start | bytes 393220
